TPU v7x, 256 devices: a whole 4x4x8 slice. The times are simulated.
256 devices in a mesh: oi: 16 (over y, x_hi, core), oj: 16 (over z, x_lo).
Axes of the slice: x: 4 (x_hi: 2, x_lo: 2; x = x_hi * 2 + x_lo), y: 4, z: 8, core: 2. Of those that a mesh axis runs over, the one named last changes fastest.
Arguments:
- amps: bfloat16 [64, 64, 32768], P('oi', 'oj'), may hold values from -6 to 6
- ladder_w: bfloat16 [2016, 2016], P('oj'), may hold values from -0.125 to 0.125
- fock: bfloat16 [64, 64], replicated, may hold values from -0.75 to 0.75
- eps_occ: float32 [64], replicated, may hold values from -2 to -0.3
- eps_pair: float32 [32768], replicated, may hold values from 0.5 to 4
Outputs:
- update: bfloat16 [64, 64, 32768], P('oi', 'oj')
All inputs are finite; a program needn't handle non-finite values.
Results may differ from a plain program's by a relative error of at most 0.0054.
Values may be sent and summed in bfloat16 or wider, within the bound.
No kernel may reach another device: no remote copies, remote signals or barrier semaphores. Data moves between devices by JAX's collectives and lax.ppermute only.
A program may use at most 128 MiB of HBM per device.

v0:
```python
import jax
import jax.numpy as jnp
import numpy as np
from jax import lax
from jax.sharding import PartitionSpec as P


def pair_tables(occ):
    first, second = np.triu_indices(occ, 1)
    upper = (first * occ + second).astype(np.int32)
    lower = (second * occ + first).astype(np.int32)
    npairs = upper.shape[0]
    expand = np.full((occ * occ,), 2 * npairs, dtype=np.int32)
    expand[upper] = np.arange(npairs, dtype=np.int32)
    expand[lower] = npairs + np.arange(npairs, dtype=np.int32)
    return (upper, lower, expand)


def divide_out(resid, energies, first_eps, second_eps):
    denom = energies[None, None, :] - first_eps[:, None, None] - second_eps[None, :, None]
    held = lax.optimization_barrier(resid)
    return (held.astype(jnp.float32) / denom).astype(jnp.bfloat16)


def on_device(amps, ladder_w, fock, eps_occ, eps_pair):
    pair_amps = lax.all_to_all(
        lax.all_to_all(amps, "oi", split_axis=2, concat_axis=0, tiled=True),
        "oj",
        split_axis=2,
        concat_axis=1,
        tiled=True,
    )
    occ = pair_amps.shape[0]
    width = pair_amps.shape[2]
    upper, lower, expand = pair_tables(occ)
    flat = pair_amps.reshape(occ * occ, width)
    anti = (flat[upper].astype(jnp.float32) - flat[lower].astype(jnp.float32)).astype(jnp.bfloat16)
    contract = (((0,), (0,)), ((), ()))
    whole_w = lax.all_gather(ladder_w, "oj", axis=0, tiled=True)
    ladder = lax.dot_general(
        whole_w, anti[:, 0 : 0 + width], contract, preferred_element_type=jnp.float32
    )
    mixed = jnp.einsum("ikp,kj->ijp", pair_amps, fock, preferred_element_type=jnp.float32)
    filler = jnp.zeros((1, width), jnp.float32)
    full = jnp.concatenate([ladder, -ladder, filler], axis=0)[expand].reshape(occ, occ, width)
    resid = (full - (mixed - jnp.transpose(mixed, (1, 0, 2)))).astype(jnp.bfloat16)
    outgoing = resid.reshape(occ, occ, 1, 1, width)
    landed = lax.all_to_all(
        lax.all_to_all(outgoing, "oi", split_axis=0, concat_axis=2, tiled=True),
        "oj",
        split_axis=1,
        concat_axis=3,
        tiled=True,
    )
    rows_i = landed.shape[0]
    rows_j = landed.shape[1]
    arrived = landed.reshape(rows_i, rows_j, landed.shape[2] * landed.shape[3] * width)
    first_eps = lax.dynamic_slice_in_dim(eps_occ, lax.axis_index("oi") * rows_i, rows_i, 0)
    second_eps = lax.dynamic_slice_in_dim(eps_occ, lax.axis_index("oj") * rows_j, rows_j, 0)
    return divide_out(arrived, eps_pair, first_eps, second_eps)


def solution(mesh):
    in_specs = (P("oi", "oj", None), P("oj", None), P(), P(), P())
    out_specs = P("oi", "oj", None)
    return jax.shard_map(
        on_device, mesh=mesh, in_specs=in_specs, out_specs=out_specs, check_vma=False
    )
```

profile of v0, /device:TPU:2, one launch (start us, length us, event | category | flops | bytes accessed | tf_op | source)
XLA Modules:
  0.0 460.0 jit_solution(2015257166413810704)
XLA Ops:
  7.3 34.8 %copy.33 = bf16[4,4,32768]{1,0,2:T(4,128)(2,1)} copy(bf16[4,4,32768]{2,1,0:T(4,128)(2,1)} %param.11) | data formatting | bytes 2097152 | tf_op args[0]
  42.1 67.7 %reshape.75 = bf16[16,2,16384]{2,1,0:T(2,128)(2,1)S(1)} reshape(bf16[32768,4,4]{2,1,0:T(4,128)(2,1)} %bitcast.50) | data formatting | bytes 2097152
  109.8 48.0 %all_to_all.69 = bf16[16,2,16384]{2,1,0:T(2,128)(2,1)S(1)} all-to-all(bf16[16,2,16384]{2,1,0:T(2,128)(2,1)S(1)} %reshape.75), channel_id=1, replica_groups=mesh['oi'=16,'oj'=16] {'oi'}, dimensions={0} | all-to-all | bytes 2097152 | tf_op jit(solution)/shard_map/all_to_all | solution.py:27
  157.7 73.1 %reshape.76 = bf16[32768,4,4]{2,1,0:T(4,128)(2,1)} reshape(bf16[16,2,16384]{2,1,0:T(2,128)(2,1)S(1)} %all_to_all.69) | data formatting | bytes 2097152
  230.8 47.0 %copy.34 = bf16[4,4,16,2048]{3,1,0,2:T(4,128)(2,1)S(1)} copy(bf16[4,4,16,2048]{1,0,3,2:T(4,128)(2,1)} %bitcast.49) | data formatting | bytes 2097152 | tf_op jit(solution)/shard_map/all_to_all | solution.py:27
  277.8 1.7 copy.35
  279.5 2.2 reshape.77
  281.8 8.8 %all-to-all-start.1 = ((bf16[16,2,16384]{2,1,0:T(2,128)(2,1)}), bf16[16,2,16384]{2,1,0:T(2,128)(2,1)S(1)}, u32[]{:S(2)}, u32[]{:S(2)}) async-start(bf16[16,2,16384]{2,1,0:T(2,128)(2,1)} %reshape.77), calls=%async_computation.1 | async-start | bytes 2097152 | tf_op jit(solution)/shard_map/all_to_all | solution.py:26
  290.7 27.0 %all-to-all-done.1 = bf16[16,2,16384]{2,1,0:T(2,128)(2,1)S(1)} async-done(((bf16[16,2,16384]{2,1,0:T(2,128)(2,1)}), bf16[16,2,16384]{2,1,0:T(2,128)(2,1)S(1)}, u32[]{:S(2)}, u32[]{:S(2)}) %all-to-all-start.1) | async-done | bytes 1048608 | tf_op jit(solution)/shard_map/all_to_all | solution.py:26
  320.5 6.3 %gather_fusion.1 = bf16[2016,128]{1,0:T(8,128)(2,1)S(1)} fusion(bf16[4096,128]{1,0:T(8,128)(2,1)S(1)} %bitcast.51, s32[2048]{0:T(1024)S(1)} %pad_clamp_fusion), kind=kCustom, calls=%fused_computation.1 | custom fusion | bytes 1040256 | tf_op jit(solution)/shard_map/gather | solution.py:37
  326.8 6.3 %gather_fusion = bf16[2016,128]{1,0:T(8,128)(2,1)S(1)} fusion(bf16[4096,128]{1,0:T(8,128)(2,1)S(1)} %bitcast.52, s32[2048]{0:T(1024)S(1)} %pad_clamp_fusion.1), kind=kCustom, calls=%fused_computation | custom fusion | bytes 1040256 | tf_op jit(solution)/shard_map/gather | solution.py:37
  333.2 1.8 fusion.4
  335.0 14.1 %copy.37 = bf16[16,126,2016]{1,0,2:T(8,128)(2,1)} copy(bf16[16,126,2016]{1,2,0:T(8,128)(2,1)} %all-gather.3.cloned.1.call-done) | data formatting | bytes 16257024 | tf_op jit(solution)/shard_map/all_gather | solution.py:39
  349.1 15.7 %reshape.72 = bf16[2016,2016]{0,1:T(8,128)(2,1)} reshape(bf16[16,126,2016]{1,0,2:T(8,128)(2,1)} %copy.37) | data formatting | bytes 16257024
  364.8 5.7 %fusion.7 = (f32[2016,128]{1,0:T(8,128)S(1)}, f32[2016,128]{1,0:T(8,128)S(1)}) fusion(bf16[2016,2016]{0,1:T(8,128)(2,1)} %reshape.72, bf16[2016,128]{1,0:T(8,128)(2,1)S(1)} %gather_fusion.1, bf16[2016,128]{1,0:T(8,128)(2,1)S(1)} %gather_fusion), kind=kOutput, calls=%fused_computation.20 | convolution fusion | flops 1041739776 | bytes 11225088 | tf_op jit(solution)/shard_map/dot_general | solution.py:40
  370.6 3.1 maximum_maximum_fusion
  373.7 14.2 %gather_fusion.2 = f32[4096,128]{1,0:T(8,128)} fusion(f32[4033,128]{1,0:T(8,128)S(1)} %maximum_maximum_fusion, s32[4096]{0:T(1024)S(1)} %broadcast_clamp_fusion), kind=kCustom, calls=%fused_computation.2 | custom fusion | bytes 4210688 | tf_op jit(solution)/shard_map/gather | solution.py:45
  387.8 5.2 %fusion.3 = bf16[64,64,1,1,128]{4,0,1,3,2:T(8,128)(2,1)S(1)} fusion(f32[64,64,128]{2,0,1:T(8,128)} %fusion.4, f32[64,64,128]{2,1,0:T(8,128)} %bitcast.56), kind=kLoop, calls=%fused_computation.10 | loop fusion | flops 1572864 | bytes 5242880 | tf_op jit(solution)/shard_map/reshape | solution.py:47
  394.7 3.7 all-to-all-start.2
  398.5 17.9 %all-to-all-done.2 = bf16[64,64,1,1,128]{4,1,3,2,0:T(8,128)(2,1)S(1)} async-done(((bf16[64,64,1,1,128]{4,1,3,2,0:T(8,128)(2,1)}), bf16[64,64,1,1,128]{4,1,3,2,0:T(8,128)(2,1)S(1)}, u32[]{:S(2)}, u32[]{:S(2)}) %all-to-all-start.2) | async-done | bytes 1048608 | tf_op jit(solution)/shard_map/all_to_all | solution.py:49
  416.4 1.8 copy.53
  418.2 4.9 %all-to-all-start.3 = ((bf16[4,64,16,1,128]{4,0,2,3,1:T(4,128)(2,1)}), bf16[4,64,16,1,128]{4,0,2,3,1:T(4,128)(2,1)S(1)}, u32[]{:S(2)}, u32[]{:S(2)}) async-start(bf16[4,64,16,1,128]{4,0,2,3,1:T(4,128)(2,1)} %bitcast.48), calls=%async_computation.3 | async-start | bytes 2097152 | tf_op jit(solution)/shard_map/all_to_all | solution.py:48
  423.2 27.1 %all-to-all-done.3 = bf16[4,64,16,1,128]{4,0,2,3,1:T(4,128)(2,1)S(1)} async-done(((bf16[4,64,16,1,128]{4,0,2,3,1:T(4,128)(2,1)}), bf16[4,64,16,1,128]{4,0,2,3,1:T(4,128)(2,1)S(1)}, u32[]{:S(2)}, u32[]{:S(2)}) %all-to-all-start.3) | async-done | bytes 1048608 | tf_op jit(solution)/shard_map/all_to_all | solution.py:48
  451.4 1.8 fusion.2
  (26 shorter events, 6.5 us)
Async XLA Ops:
  6.5 326.6 %copy-start = (bf16[64,64]{1,0:T(8,128)(2,1)S(1)}, bf16[64,64]{1,0:T(8,128)(2,1)}, u32[]{:S(2)}) copy-start(bf16[64,64]{1,0:T(8,128)(2,1)} %param.13) | copy-start | bytes 24580
  6.5 328.4 %all-gather.3.cloned.1.call-start = ((), (), s32[]{:S(2)}) async-start(), calls=%async_computation.4 | async-start | bytes 8773632 | tf_op jit(solution)/shard_map/all_gather | solution.py:39
  279.5 11.2 %copy-start.4 = (s32[2016]{0:T(1024)S(1)}, s32[2016]{0:T(1024)}, u32[]{:S(2)}) copy-start(s32[2016]{0:T(1024)} %constant.39) | copy-start | bytes 24196
  279.5 11.2 %copy-start.3 = (s32[2016]{0:T(1024)S(1)}, s32[2016]{0:T(1024)}, u32[]{:S(2)}) copy-start(s32[2016]{0:T(1024)} %constant.38) | copy-start | bytes 24196
  279.5 11.2 %copy-start.2 = (s32[4096]{0:T(1024)S(1)}, s32[4096]{0:T(1024)}, u32[]{:S(2)}) copy-start(s32[4096]{0:T(1024)} %constant.40) | copy-start | bytes 49156
  281.8 36.0 %all-to-all-start.1 = ((bf16[16,2,16384]{2,1,0:T(2,128)(2,1)}), bf16[16,2,16384]{2,1,0:T(2,128)(2,1)S(1)}, u32[]{:S(2)}, u32[]{:S(2)}) async-start(bf16[16,2,16384]{2,1,0:T(2,128)(2,1)} %reshape.77), calls=%async_computation.1 | async-start | bytes 2097152 | tf_op jit(solution)/shard_map/all_to_all | solution.py:26
  393.1 5.3 %copy-start.5 = (f32[64]{0:T(128)S(1)}, f32[64]{0:T(128)}, u32[]{:S(2)}) copy-start(f32[64]{0:T(128)} %param.14) | copy-start | bytes 772
  394.7 21.7 %all-to-all-start.2 = ((bf16[64,64,1,1,128]{4,1,3,2,0:T(8,128)(2,1)}), bf16[64,64,1,1,128]{4,1,3,2,0:T(8,128)(2,1)S(1)}, u32[]{:S(2)}, u32[]{:S(2)}) async-start(bf16[64,64,1,1,128]{4,1,3,2,0:T(8,128)(2,1)} %copy.41), calls=%async_computation.2 | async-start | bytes 2097152 | tf_op jit(solution)/shard_map/all_to_all | solution.py:49
  416.4 6.7 %copy-start.1 = (f32[32768]{0:T(1024)S(1)}, f32[32768]{0:T(1024)}, u32[]{:S(2)}) copy-start(f32[32768]{0:T(1024)} %param.15) | copy-start | bytes 393220
  418.2 32.1 %all-to-all-start.3 = ((bf16[4,64,16,1,128]{4,0,2,3,1:T(4,128)(2,1)}), bf16[4,64,16,1,128]{4,0,2,3,1:T(4,128)(2,1)S(1)}, u32[]{:S(2)}, u32[]{:S(2)}) async-start(bf16[4,64,16,1,128]{4,0,2,3,1:T(4,128)(2,1)} %bitcast.48), calls=%async_computation.3 | async-start | bytes 2097152 | tf_op jit(solution)/shard_map/all_to_all | solution.py:48
Sparse Core Ops, SparseCore 0:
  9.1 192.8 all-gather.2
where the time goes:
time: 465 us; the launch traced here: 460 us
  local copies, waits for them, and re-layouts  291 us (63%)
  waiting for transfers between devices  72.7 us (16%)
  blocking collectives  48 us (10%)
  starting transfers between devices  17.4 us (4%)
  between operations  13.6 us (3%)
  other arithmetic  10.3 us (2%)
  matrix products  7.52 us (2%)
    unnamed x18, local copies, waits for them, and re-layouts  195 us
    all_to_all x2, local copies, waits for them, and re-layouts, on_device(): lax.all_to_all(amps, 'oi', split_axis=2, concat_axis=0, tiled=True)  48.7 us
    all_to_all x1, blocking collectives, on_device(): lax.all_to_all(amps, 'oi', split_axis=2, concat_axis=0, tiled=True)  48 us
    all_to_all x1, waiting for transfers between devices, on_device(): lax.all_to_all(lax.all_to_all(outgoing, 'oi', split_axis=0, concat_axis=2...  27.1 us
    all_to_all x1, waiting for transfers between devices, on_device(): lax.all_to_all(lax.all_to_all(amps, 'oi', split_axis=2, concat_axis=0, ti...  27 us
    all_to_all x1, waiting for transfers between devices, on_device(): lax.all_to_all(outgoing, 'oi', split_axis=0, concat_axis=2, tiled=True)  17.9 us
    gather x1, local copies, waits for them, and re-layouts, on_device(): jnp.concatenate([ladder, -ladder, filler], axis=0)[expand]  14.2 us
    all_gather x1, local copies, waits for them, and re-layouts, on_device(): whole_w = lax.all_gather(ladder_w, 'oj', axis=0, tiled=True)  14.1 us
  transfers between devices with their start and end apart: 4, of which 3 were waited for; matrix products, arithmetic and copies ran while one was open for 53% of the time, Pallas kernels for 0%

commit v1 on v0

--- a/solution.py
+++ b/solution.py
@@ -36,7 +36,13 @@
     flat = pair_amps.reshape(occ * occ, width)
     anti = (flat[upper].astype(jnp.float32) - flat[lower].astype(jnp.float32)).astype(jnp.bfloat16)
     contract = (((0,), (0,)), ((), ()))
-    whole_w = lax.all_gather(ladder_w, "oj", axis=0, tiled=True)
+
+    def list_turns(view, d_out):
+        return jnp.concatenate(
+            lax.all_to_all(jnp.stack(lax.axis_size("oj") * [view]), "oj", 0, 0), axis=d_out
+        )
+
+    whole_w = list_turns(ladder_w, 0)
     ladder = lax.dot_general(
         whole_w, anti[:, 0 : 0 + width], contract, preferred_element_type=jnp.float32
     )

time: 465 us -> 608 us (1.31)
  waiting for transfers between devices: 72.7 us -> 212 us
  between operations: 13.6 us -> 0.18 us
  blocking collectives: 48 us -> 60 us
    all_to_all x1, waiting for transfers between devices: 27 us -> 168 us  [list_turns(): lax.all_to_all(jnp.stack(lax.axis_size('oj') * [view]), 'oj', 0, 0)]
    all_to_all x0 -> x1, blocking collectives: none -> 36.1 us  [on_device(): lax.all_to_all(lax.all_to_all(amps, 'oi', split_axis=2, concat_axis=0, ti...]
    all_to_all x1, blocking collectives: 48 us -> 23.9 us  [on_device(): lax.all_to_all(amps, 'oi', split_axis=2, concat_axis=0, tiled=True)]
    unnamed x18 -> x19, local copies, waits for them, and re-layouts: 195 us -> 178 us
    reshape x0 -> x1, local copies, waits for them, and re-layouts: none -> 15.7 us  [list_turns(): jnp.concatenate(lax.all_to_all(jnp.stack(lax.axis_size('oj') * [view]), '...]
    all_gather x1 -> x0, local copies, waits for them, and re-layouts: 14.1 us -> none  [on_device(): whole_w = lax.all_gather(ladder_w, 'oj', axis=0, tiled=True)]
    all_to_all x0 -> x1, local copies, waits for them, and re-layouts: none -> 14.1 us  [list_turns(): lax.all_to_all(jnp.stack(lax.axis_size('oj') * [view]), 'oj', 0, 0)]
  transfers between devices with their start and end apart: 4 -> 3, of which waited for: 3 -> 3; matrix products, arithmetic and copies ran while one was open for 53% -> 3% of each run, Pallas kernels for 0% -> 0%
where the time goes in v1:
time: 608 us; the launch traced here: 602 us
  local copies, waits for them, and re-layouts  294 us (48%)
  waiting for transfers between devices  212 us (35%)
  blocking collectives  60 us (10%)
  starting transfers between devices  18.1 us (3%)
  other arithmetic  10.3 us (2%)
  matrix products  7.53 us (1%)
    unnamed x19, local copies, waits for them, and re-layouts  178 us
    all_to_all x1, waiting for transfers between devices, list_turns(): lax.all_to_all(jnp.stack(lax.axis_size('oj') * [view]), 'oj', 0, 0)  168 us
    all_to_all x2, local copies, waits for them, and re-layouts, on_device(): lax.all_to_all(amps, 'oi', split_axis=2, concat_axis=0, tiled=True)  48.7 us
    all_to_all x1, blocking collectives, on_device(): lax.all_to_all(lax.all_to_all(amps, 'oi', split_axis=2, concat_axis=0, ti...  36.1 us
    all_to_all x1, waiting for transfers between devices, on_device(): lax.all_to_all(lax.all_to_all(outgoing, 'oi', split_axis=0, concat_axis=2...  26.8 us
    all_to_all x1, blocking collectives, on_device(): lax.all_to_all(amps, 'oi', split_axis=2, concat_axis=0, tiled=True)  23.9 us
    all_to_all x1, waiting for transfers between devices, on_device(): lax.all_to_all(outgoing, 'oi', split_axis=0, concat_axis=2, tiled=True)  17.9 us
    reshape x1, local copies, waits for them, and re-layouts, list_turns(): jnp.concatenate(lax.all_to_all(jnp.stack(lax.axis_size('oj') * [view]), '...  15.7 us
  transfers between devices with their start and end apart: 3, of which 3 were waited for; matrix products, arithmetic and copies ran while one was open for 3% of the time, Pallas kernels for 0%

profile of v1, /device:TPU:2, one launch (start us, length us, event | category | flops | bytes accessed | tf_op | source)
XLA Modules:
  0.0 602.5 jit_solution(1943676671823965468)
XLA Ops:
  0.0 34.8 %copy.33 = bf16[4,4,32768]{1,0,2:T(4,128)(2,1)} copy(bf16[4,4,32768]{2,1,0:T(4,128)(2,1)} %param.11) | data formatting | bytes 2097152 | tf_op args[0]
  34.8 67.6 %reshape.79 = bf16[16,2,16384]{2,1,0:T(2,128)(2,1)S(1)} reshape(bf16[32768,4,4]{2,1,0:T(4,128)(2,1)} %bitcast.49) | data formatting | bytes 2097152
  102.5 23.9 %all_to_all.74 = bf16[16,2,16384]{2,1,0:T(2,128)(2,1)S(1)} all-to-all(bf16[16,2,16384]{2,1,0:T(2,128)(2,1)S(1)} %reshape.79), channel_id=1, replica_groups=mesh['oi'=16,'oj'=16] {'oi'}, dimensions={0} | all-to-all | bytes 2097152 | tf_op jit(solution)/shard_map/all_to_all | solution.py:27
  126.4 73.1 %reshape.80 = bf16[32768,4,4]{2,1,0:T(4,128)(2,1)} reshape(bf16[16,2,16384]{2,1,0:T(2,128)(2,1)S(1)} %all_to_all.74) | data formatting | bytes 2097152
  199.4 47.0 %copy.34 = bf16[4,4,16,2048]{3,1,0,2:T(4,128)(2,1)S(1)} copy(bf16[4,4,16,2048]{1,0,3,2:T(4,128)(2,1)} %bitcast.48) | data formatting | bytes 2097152 | tf_op jit(solution)/shard_map/all_to_all | solution.py:27
  249.6 36.1 %all_to_all.75 = bf16[16,2,16384]{2,1,0:T(2,128)(2,1)S(1)} all-to-all(bf16[16,2,16384]{2,1,0:T(2,128)(2,1)S(1)} %reshape.81), channel_id=1, replica_groups=mesh['oi'=16,'oj'=16] {'oj'}, dimensions={0} | all-to-all | bytes 2097152 | tf_op jit(solution)/shard_map/all_to_all | solution.py:26
  285.7 4.2 stack.2
  289.9 6.3 %all-to-all-start.2 = ((bf16[16,126,2016]{1,2,0:T(8,128)(2,1)}), bf16[16,126,2016]{1,2,0:T(8,128)(2,1)}, u32[]{:S(2)}, u32[]{:S(2)}) async-start(bf16[16,126,2016]{1,2,0:T(8,128)(2,1)} %stack.2), calls=%async_computation.2 | async-start | bytes 16515072 | tf_op jit(solution)/shard_map/all_to_all | solution.py:42
  299.1 6.3 %gather_fusion.1 = bf16[2016,128]{1,0:T(8,128)(2,1)S(1)} fusion(bf16[4096,128]{1,0:T(8,128)(2,1)S(1)} %bitcast.50, s32[2048]{0:T(1024)S(1)} %pad_clamp_fusion), kind=kCustom, calls=%fused_computation.1 | custom fusion | bytes 1040256 | tf_op jit(solution)/shard_map/gather | solution.py:37
  305.5 6.3 %gather_fusion = bf16[2016,128]{1,0:T(8,128)(2,1)S(1)} fusion(bf16[4096,128]{1,0:T(8,128)(2,1)S(1)} %bitcast.51, s32[2048]{0:T(1024)S(1)} %pad_clamp_fusion.1), kind=kCustom, calls=%fused_computation | custom fusion | bytes 1040256 | tf_op jit(solution)/shard_map/gather | solution.py:37
  311.9 1.8 fusion.4
  313.7 167.7 %all-to-all-done.2 = bf16[16,126,2016]{1,2,0:T(8,128)(2,1)} async-done(((bf16[16,126,2016]{1,2,0:T(8,128)(2,1)}), bf16[16,126,2016]{1,2,0:T(8,128)(2,1)}, u32[]{:S(2)}, u32[]{:S(2)}) %all-to-all-start.2) | async-done | bytes 8128544 | tf_op jit(solution)/shard_map/all_to_all | solution.py:42
  481.3 14.1 %copy.37 = bf16[16,126,2016]{1,0,2:T(8,128)(2,1)} copy(bf16[16,126,2016]{1,2,0:T(8,128)(2,1)} %all-to-all-done.2) | data formatting | bytes 16257024 | tf_op jit(solution)/shard_map/all_to_all | solution.py:42
  495.4 15.7 %reshape.49 = bf16[2016,2016]{0,1:T(8,128)(2,1)} reshape(bf16[16,126,2016]{1,0,2:T(8,128)(2,1)} %copy.37) | data formatting | bytes 16257024 | tf_op jit(solution)/shard_map/reshape | solution.py:41
  511.2 5.7 fusion.7
  516.9 3.1 maximum_maximum_fusion
  520.0 14.2 %gather_fusion.2 = f32[4096,128]{1,0:T(8,128)} fusion(f32[4033,128]{1,0:T(8,128)S(1)} %maximum_maximum_fusion, s32[4096]{0:T(1024)S(1)} %broadcast_clamp_fusion), kind=kCustom, calls=%fused_computation.2 | custom fusion | bytes 4210688 | tf_op jit(solution)/shard_map/gather | solution.py:51
  534.2 5.2 fusion.3
  541.1 3.9 all-to-all-start.3
  545.1 17.9 %all-to-all-done.3 = bf16[64,64,1,1,128]{4,1,3,2,0:T(8,128)(2,1)S(1)} async-done(((bf16[64,64,1,1,128]{4,1,3,2,0:T(8,128)(2,1)}), bf16[64,64,1,1,128]{4,1,3,2,0:T(8,128)(2,1)S(1)}, u32[]{:S(2)}, u32[]{:S(2)}) %all-to-all-start.3) | async-done | bytes 1048608 | tf_op jit(solution)/shard_map/all_to_all | solution.py:55
  563.0 1.8 copy.53
  564.8 7.9 %all-to-all-start.4 = ((bf16[4,64,16,1,128]{4,0,2,3,1:T(4,128)(2,1)}), bf16[4,64,16,1,128]{4,0,2,3,1:T(4,128)(2,1)S(1)}, u32[]{:S(2)}, u32[]{:S(2)}) async-start(bf16[4,64,16,1,128]{4,0,2,3,1:T(4,128)(2,1)} %bitcast.47), calls=%async_computation.4 | async-start | bytes 2097152 | tf_op jit(solution)/shard_map/all_to_all | solution.py:54
  572.8 26.8 %all-to-all-done.4 = bf16[4,64,16,1,128]{4,0,2,3,1:T(4,128)(2,1)S(1)} async-done(((bf16[4,64,16,1,128]{4,0,2,3,1:T(4,128)(2,1)}), bf16[4,64,16,1,128]{4,0,2,3,1:T(4,128)(2,1)S(1)}, u32[]{:S(2)}, u32[]{:S(2)}) %all-to-all-start.4) | async-done | bytes 1048608 | tf_op jit(solution)/shard_map/all_to_all | solution.py:54
  600.7 1.8 fusion.2
  (27 shorter events, 9.0 us)
Async XLA Ops:
  0.0 311.8 %copy-start = (bf16[64,64]{1,0:T(8,128)(2,1)S(1)}, bf16[64,64]{1,0:T(8,128)(2,1)}, u32[]{:S(2)}) copy-start(bf16[64,64]{1,0:T(8,128)(2,1)} %param.13) | copy-start | bytes 24580
  249.6 36.1 %copy-start.1 = (bf16[126,2016]{0,1:T(8,128)(2,1)S(1)}, bf16[126,2016]{0,1:T(8,128)(2,1)}, u32[]{:S(2)}) copy-start(bf16[126,2016]{0,1:T(8,128)(2,1)} %param.12) | copy-start | bytes 1524100
  289.9 6.4 %copy-start.5 = (s32[2016]{0:T(1024)S(1)}, s32[2016]{0:T(1024)}, u32[]{:S(2)}) copy-start(s32[2016]{0:T(1024)} %constant.39) | copy-start | bytes 24196
  289.9 6.4 %copy-start.4 = (s32[2016]{0:T(1024)S(1)}, s32[2016]{0:T(1024)}, u32[]{:S(2)}) copy-start(s32[2016]{0:T(1024)} %constant.38) | copy-start | bytes 24196
  289.9 6.5 %copy-start.3 = (s32[4096]{0:T(1024)S(1)}, s32[4096]{0:T(1024)}, u32[]{:S(2)}) copy-start(s32[4096]{0:T(1024)} %constant.40) | copy-start | bytes 49156
  289.9 191.4 %all-to-all-start.2 = ((bf16[16,126,2016]{1,2,0:T(8,128)(2,1)}), bf16[16,126,2016]{1,2,0:T(8,128)(2,1)}, u32[]{:S(2)}, u32[]{:S(2)}) async-start(bf16[16,126,2016]{1,2,0:T(8,128)(2,1)} %stack.2), calls=%async_computation.2 | async-start | bytes 16515072 | tf_op jit(solution)/shard_map/all_to_all | solution.py:42
  539.4 5.6 copy-start.6
  541.1 22.0 %all-to-all-start.3 = ((bf16[64,64,1,1,128]{4,1,3,2,0:T(8,128)(2,1)}), bf16[64,64,1,1,128]{4,1,3,2,0:T(8,128)(2,1)S(1)}, u32[]{:S(2)}, u32[]{:S(2)}) async-start(bf16[64,64,1,1,128]{4,1,3,2,0:T(8,128)(2,1)} %copy.41), calls=%async_computation.3 | async-start | bytes 2097152 | tf_op jit(solution)/shard_map/all_to_all | solution.py:55
  563.0 9.7 %copy-start.2 = (f32[32768]{0:T(1024)S(1)}, f32[32768]{0:T(1024)}, u32[]{:S(2)}) copy-start(f32[32768]{0:T(1024)} %param.15) | copy-start | bytes 393220
  564.8 34.8 %all-to-all-start.4 = ((bf16[4,64,16,1,128]{4,0,2,3,1:T(4,128)(2,1)}), bf16[4,64,16,1,128]{4,0,2,3,1:T(4,128)(2,1)S(1)}, u32[]{:S(2)}, u32[]{:S(2)}) async-start(bf16[4,64,16,1,128]{4,0,2,3,1:T(4,128)(2,1)} %bitcast.47), calls=%async_computation.4 | async-start | bytes 2097152 | tf_op jit(solution)/shard_map/all_to_all | solution.py:54
